TPU v7x, 32 devices: a whole 2x2x4 slice. The times are simulated.
32 devices in a mesh: group: 2 (over y), ctx: 4 (over z), head: 2 (over x), sub: 2 (over core).
Axes of the slice: x: 2, y: 2, z: 4, core: 2. Of those that a mesh axis runs over, the one named last changes fastest.
Arguments:
- queries: bfloat16 [4, 4096, 128], P(('head', 'sub'), ('group', 'ctx')), parts along dimension 1, may hold values from -18 to 18
- keys: bfloat16 [4, 4096, 128], P(('head', 'sub'), ('group', 'ctx')), parts along dimension 1, may hold values from -6 to 6
- values: bfloat16 [4, 4096, 128], P(('head', 'sub'), ('group', 'ctx')), parts along dimension 1, may hold values from -6 to 6
- stick_offset: float32 [4], P(('head', 'sub')), may hold values from -14 to -7
Outputs:
- attended: bfloat16 [4, 4096, 128], P(('head', 'sub'), ('group', 'ctx')), parts along dimension 1
There are 2 independent parts, one for each index of `group`. A program takes and returns all parts, laid end to end along the dimension named above; an argument that names none is the same for every part. Nothing has to cross between parts.
All inputs are finite; a program needn't handle non-finite values.
Results may differ from a plain program's by a relative error of at most 0.0049.
Values may be sent and summed in bfloat16 or wider, within the bound.
No kernel may reach another device: no remote copies, remote signals or barrier semaphores. Data moves between devices by JAX's collectives and lax.ppermute only.
A program may use at most 64 MiB of HBM per device.

v0:
```python
import math
import jax
import jax.numpy as jnp
from jax import lax
from jax.sharding import PartitionSpec as P


def shifted(block, axis, distance):
    devices = range(lax.axis_size(axis))
    route = [((i - distance) % len(devices), i) for i in devices]
    return lax.ppermute(block, axis, route)


def shard_terms(qrows, qstart, kblock, vblock, kstart, offset):
    count_rows = qrows.shape[0]
    count_keys = kblock.shape[0]
    width = qrows.shape[1]
    scale = 1.0 / math.sqrt(width)

    def compute(unused):
        score = (
            lax.dot_general(
                qrows, kblock, (((1,), (1,)), ((), ())), preferred_element_type=jnp.float32
            )
            * scale
            + offset
        )
        qpos = qstart + lax.iota(jnp.int32, count_rows)
        kpos = kstart + lax.iota(jnp.int32, count_keys)
        live = kpos[None, :] < qpos[:, None]
        spent = jnp.where(live, jax.nn.softplus(score), 0.0)
        total = jnp.sum(spent, axis=1)
        later = lax.cumsum(spent, axis=1, reverse=True) - spent
        weight = jnp.where(live, jnp.exp(jax.nn.log_sigmoid(score) - later), 0.0).astype(
            jnp.bfloat16
        )
        return (total, jnp.dot(weight, vblock, preferred_element_type=jnp.float32))

    def nothing(unused):
        return (jnp.zeros((count_rows,), jnp.float32), jnp.zeros((count_rows, width), jnp.float32))

    return lax.cond(qstart + count_rows > kstart, compute, nothing, 0)


def one_head(q_own, k_own, v_own, offset):
    rows, width = q_own.shape
    count = lax.axis_size("ctx")
    place = lax.axis_index("ctx")
    own_start = place * rows
    gathered = lax.all_gather(q_own, "ctx", axis=0, tiled=True).reshape(count, rows, width)

    def advance(step, message):
        summed, spent_sum = message
        block = (place + step + 1) % count
        qrows = lax.dynamic_index_in_dim(gathered, block, 0, keepdims=False)
        total, partial_value = shard_terms(qrows, block * rows, k_own, v_own, own_start, offset)
        summed = summed + jnp.exp(-spent_sum)[:, None] * partial_value
        spent_sum = spent_sum + total
        return shifted((summed, spent_sum), "ctx", -1)

    start_message = (jnp.zeros((rows, width), jnp.float32), jnp.zeros((rows,), jnp.float32))
    summed, spent_sum = lax.fori_loop(0, count - 1, advance, start_message)
    total, partial_value = shard_terms(q_own, own_start, k_own, v_own, own_start, offset)
    merged = partial_value + jnp.exp(-total)[:, None] * summed
    return merged.astype(jnp.bfloat16)


def on_device(queries, keys, values, stick_offset):
    results = [one_head(queries[0], keys[0], values[0], stick_offset[0])]
    return jnp.stack(results, axis=0)


def solution(mesh):
    placed = (
        P(("head", "sub"), ("group", "ctx"), None),
        P(("head", "sub"), ("group", "ctx"), None),
        P(("head", "sub"), ("group", "ctx"), None),
        P(("head", "sub")),
    )
    return jax.shard_map(
        on_device,
        mesh=mesh,
        in_specs=placed,
        out_specs=P(("head", "sub"), ("group", "ctx"), None),
        check_vma=False,
    )
```

profile of v0, /device:TPU:0, one launch (start us, length us, event | category | flops | bytes accessed | tf_op | source)
XLA Modules:
  0.0 75.3 jit_solution(1740217966002129003)
XLA Ops:
  0.0 9.7 %conditional.2 = (f32[512]{0:T(512)S(1)}, f32[512,128]{1,0:T(8,128)S(1)}) conditional(s32[]{:T(128)} %convert_element_type.23, () %tuple.48, (s32[]{:T(128)}, bf16[512,128]{1,0:T(8,128)(2,1)}, bf16[512,128]{1,0:T(8,128)(2,1)}, f32[]{:T(128)}, bf16[512,128]{1,0:T(8,128)(2,1)}) %tuple.82), branch_computations={%region_0.1_spmd, %region_1.5_spmd} | conditional | flops 175906304 | bytes 12814392 | solution.py:42
  0.0 2.5 %compare_select_fusion.3 = (f32[512,512]{0,1:T(8,128)S(1)}, f32[512,512]{0,1:T(8,128)S(1)}) fusion(s32[512]{0:T(512)S(1)} %iota_add_fusion, f32[]{:T(128)} %get-tuple-element.273, bf16[512,128]{1,0:T(8,128)(2,1)} %get-tuple-element.271, bf16[512,128]{1,0:T(8,128)(2,1)} %get-tuple-element.272), kind=kOutput, calls=%fused_computation.5 | convolution fusion | flops 69730304 | bytes 2361348 | tf_op jit(solution)/shard_map/cond/branch_1_fun/dot_general | solution.py:22
  2.5 4.8 %fusion.5 = f32[512,4,128]{0,1,2:T(4,128)S(1)} fusion(f32[512,4,128]{0,2,1:T(8,128)S(1)} %bitcast.47), kind=kOutput, calls=%fused_computation.11 | output fusion | flops 33292288 | bytes 2097152 | tf_op jit(solution)/shard_map/reduce-window.2
  7.8 1.5 %fusion.1 = (bf16[512,512]{0,1:T(8,128)(2,1)S(1)}, f32[512]{0:T(512)S(1)}) fusion(f32[512,4,128]{0,2,1:T(8,128)S(1)} %copy.6, f32[512,512]{0,1:T(8,128)S(1)} %get-tuple-element.321, s32[512]{0:T(512)S(1)} %iota_add_fusion), kind=kLoop, calls=%fused_computation.6 | loop fusion | flops 5504512 | bytes 2625536 | tf_op jit(solution)/shard_map/cond/branch_1_fun/convert_element_type | solution.py:34
  9.7 17.8 %all-gather = bf16[1,2048,128]{2,1,0:T(8,128)(2,1)S(1)} all-gather(bf16[1,512,128]{2,1,0:T(8,128)(2,1)} %param.10), channel_id=2, replica_groups=mesh['group'=2,'ctx'=4,'head'=2,'sub'=2] {'ctx'}, dimensions={1}, use_global_device_ids=true | all-gather | bytes 655360 | tf_op jit(solution)/shard_map/all_gather | solution.py:50
  27.5 0.9 %copy-done = bf16[1,512,128]{2,1,0:T(8,128)(2,1)S(1)} copy-done((bf16[1,512,128]{2,1,0:T(8,128)(2,1)S(1)}, bf16[1,512,128]{2,1,0:T(8,128)(2,1)}, u32[]{:S(2)}) %copy-start) | copy-done | bytes 131096
  28.4 46.1 %while.17 = (s32[]{:T(128)}, f32[512,128]{1,0:T(8,128)S(1)}, f32[512]{0:T(512)S(1)}, s32[]{:T(128)}, s32[]{:T(128)}, /*index=5*/bf16[4,512,128]{2,1,0:T(8,128)(2...) while((s32[]{:T(128)}, f32[512,128]{1,0:T(8,128)S(1)}, ...), condition=%wide.region_11.12_spmd, body=%wide.region_5.11_spmd.sunk | while | flops 176038928 | bytes 14150142 | solution.py:62
  28.4 8.7 %conditional.4 = (f32[512]{0:T(512)S(1)}, f32[512,128]{1,0:T(8,128)S(1)}) conditional(s32[]{:T(128)} %convert_element_type.31, () %tuple.69, (s32[]{:T(128)}, s32[]{:T(128)}, s32[]{:T(128)}, bf16[4,512,128]{2,1,0:T(8,128)(2,1)S(1)}, bf16[512,128]{1,0:T(8,128)(2,1)S(1)}, /*index=5*/f32[]{:T(128)}, bf16[512,128]{1,0:T(8,128)(2,1)S(1)}) %tuple.70), branch_computations={%region_6.6_spmd, %region_7.10_spmd} | conditional | flops 175906816 | bytes 12296262 | solution.py:42
  28.4 1.5 %compare_select_fusion.7 = (f32[512,512]{0,1:T(8,128)S(1)}, f32[512,512]{0,1:T(8,128)S(1)}) fusion(s32[512]{0:T(512)S(1)} %get-tuple-element.326, s32[512]{0:T(512)S(1)} %get-tuple-element.327, f32[]{:T(128)} %get-tuple-element.280, bf16[512,128]{1,0:T(8,128)(2,1)S(1)} %get-tuple-element.279, bf16[4,512,128]{2,1,0:T(8,128)(2,1)S(1)} %get-tuple-element.277, ...), kind=kOutput, calls=%fused_computation.22 | convolution fusion | flops 69730304 | bytes 2363400 | tf_op jit(solution)/shard_map/while/body/eval_jaxpr/cond/branch_1_fun/dot_general | solution.py:22
  29.9 4.8 %fusion.13 = f32[512,4,128]{0,1,2:T(4,128)S(1)} fusion(f32[512,4,128]{0,2,1:T(8,128)S(1)} %bitcast.41), kind=kOutput, calls=%fused_computation.28 | output fusion | flops 33292288 | bytes 2097152 | tf_op jit(solution)/shard_map/reduce-window.4
  35.2 1.5 %fusion.9 = (bf16[512,512]{0,1:T(8,128)(2,1)S(1)}, f32[512]{0:T(512)S(1)}) fusion(f32[512,4,128]{0,2,1:T(8,128)S(1)} %copy.8, f32[512,512]{0,1:T(8,128)S(1)} %get-tuple-element.325, s32[512]{0:T(512)S(1)} %get-tuple-element.326, s32[512]{0:T(512)S(1)} %get-tuple-element.327), kind=kLoop, calls=%fused_computation.23 | loop fusion | flops 5504512 | bytes 2627584 | tf_op jit(solution)/shard_map/while/body/eval_jaxpr/cond/branch_1_fun/convert_element_type | solution.py:34
  37.3 2.2 %collective-permute-start.1 = (f32[512]{0:T(512)S(1)}, f32[512]{0:T(512)S(1)}, u32[]{:S(2)}, u32[]{:S(2)}) collective-permute-start(f32[512]{0:T(512)S(1)} %get-tuple-element.392), channel_id=1, source_target_pairs={{4,0},{8,4},{12,8},{0,12},{5,1},{9,5},{13,9},{1,13},{6,2},{10,6},{... | collective-permute-start | bytes 6152 | tf_op jit(solution)/shard_map/while/body/eval_jaxpr/ppermute | solution.py:11
  39.5 4.5 %collective-permute-done.1 = f32[512]{0:T(512)S(1)} collective-permute-done((f32[512]{0:T(512)S(1)}, f32[512]{0:T(512)S(1)}, u32[]{:S(2)}, u32[]{:S(2)}) %collective-permute-start.1) | collective-permute-done | bytes 2080 | tf_op jit(solution)/shard_map/while/body/eval_jaxpr/ppermute | solution.py:11
  44.0 8.7 %conditional.4 = (f32[512]{0:T(512)S(1)}, f32[512,128]{1,0:T(8,128)S(1)}) conditional(s32[]{:T(128)} %convert_element_type.31, () %tuple.69, (s32[]{:T(128)}, s32[]{:T(128)}, s32[]{:T(128)}, bf16[4,512,128]{2,1,0:T(8,128)(2,1)S(1)}, bf16[512,128]{1,0:T(8,128)(2,1)S(1)}, /*index=5*/f32[]{:T(128)}, bf16[512,128]{1,0:T(8,128)(2,1)S(1)}) %tuple.70), branch_computations={%region_6.6_spmd, %region_7.10_spmd} | conditional | flops 175906816 | bytes 12296262 | solution.py:42
  44.0 1.5 %compare_select_fusion.7 = (f32[512,512]{0,1:T(8,128)S(1)}, f32[512,512]{0,1:T(8,128)S(1)}) fusion(s32[512]{0:T(512)S(1)} %get-tuple-element.326, s32[512]{0:T(512)S(1)} %get-tuple-element.327, f32[]{:T(128)} %get-tuple-element.280, bf16[512,128]{1,0:T(8,128)(2,1)S(1)} %get-tuple-element.279, bf16[4,512,128]{2,1,0:T(8,128)(2,1)S(1)} %get-tuple-element.277, ...), kind=kOutput, calls=%fused_computation.22 | convolution fusion | flops 69730304 | bytes 2363400 | tf_op jit(solution)/shard_map/while/body/eval_jaxpr/cond/branch_1_fun/dot_general | solution.py:22
  45.5 4.8 %fusion.13 = f32[512,4,128]{0,1,2:T(4,128)S(1)} fusion(f32[512,4,128]{0,2,1:T(8,128)S(1)} %bitcast.41), kind=kOutput, calls=%fused_computation.28 | output fusion | flops 33292288 | bytes 2097152 | tf_op jit(solution)/shard_map/reduce-window.4
  50.8 1.5 %fusion.9 = (bf16[512,512]{0,1:T(8,128)(2,1)S(1)}, f32[512]{0:T(512)S(1)}) fusion(f32[512,4,128]{0,2,1:T(8,128)S(1)} %copy.8, f32[512,512]{0,1:T(8,128)S(1)} %get-tuple-element.325, s32[512]{0:T(512)S(1)} %get-tuple-element.326, s32[512]{0:T(512)S(1)} %get-tuple-element.327), kind=kLoop, calls=%fused_computation.23 | loop fusion | flops 5504512 | bytes 2627584 | tf_op jit(solution)/shard_map/while/body/eval_jaxpr/cond/branch_1_fun/convert_element_type | solution.py:34
  53.0 6.3 %collective-permute-done.1 = f32[512]{0:T(512)S(1)} collective-permute-done((f32[512]{0:T(512)S(1)}, f32[512]{0:T(512)S(1)}, u32[]{:S(2)}, u32[]{:S(2)}) %collective-permute-start.1) | collective-permute-done | bytes 2080 | tf_op jit(solution)/shard_map/while/body/eval_jaxpr/ppermute | solution.py:11
  59.3 8.7 %conditional.4 = (f32[512]{0:T(512)S(1)}, f32[512,128]{1,0:T(8,128)S(1)}) conditional(s32[]{:T(128)} %convert_element_type.31, () %tuple.69, (s32[]{:T(128)}, s32[]{:T(128)}, s32[]{:T(128)}, bf16[4,512,128]{2,1,0:T(8,128)(2,1)S(1)}, bf16[512,128]{1,0:T(8,128)(2,1)S(1)}, /*index=5*/f32[]{:T(128)}, bf16[512,128]{1,0:T(8,128)(2,1)S(1)}) %tuple.70), branch_computations={%region_6.6_spmd, %region_7.10_spmd} | conditional | flops 175906816 | bytes 12296262 | solution.py:42
  59.3 1.5 %compare_select_fusion.7 = (f32[512,512]{0,1:T(8,128)S(1)}, f32[512,512]{0,1:T(8,128)S(1)}) fusion(s32[512]{0:T(512)S(1)} %get-tuple-element.326, s32[512]{0:T(512)S(1)} %get-tuple-element.327, f32[]{:T(128)} %get-tuple-element.280, bf16[512,128]{1,0:T(8,128)(2,1)S(1)} %get-tuple-element.279, bf16[4,512,128]{2,1,0:T(8,128)(2,1)S(1)} %get-tuple-element.277, ...), kind=kOutput, calls=%fused_computation.22 | convolution fusion | flops 69730304 | bytes 2363400 | tf_op jit(solution)/shard_map/while/body/eval_jaxpr/cond/branch_1_fun/dot_general | solution.py:22
  60.8 4.8 %fusion.13 = f32[512,4,128]{0,1,2:T(4,128)S(1)} fusion(f32[512,4,128]{0,2,1:T(8,128)S(1)} %bitcast.41), kind=kOutput, calls=%fused_computation.28 | output fusion | flops 33292288 | bytes 2097152 | tf_op jit(solution)/shard_map/reduce-window.4
  66.1 1.5 %fusion.9 = (bf16[512,512]{0,1:T(8,128)(2,1)S(1)}, f32[512]{0:T(512)S(1)}) fusion(f32[512,4,128]{0,2,1:T(8,128)S(1)} %copy.8, f32[512,512]{0,1:T(8,128)S(1)} %get-tuple-element.325, s32[512]{0:T(512)S(1)} %get-tuple-element.326, s32[512]{0:T(512)S(1)} %get-tuple-element.327), kind=kLoop, calls=%fused_computation.23 | loop fusion | flops 5504512 | bytes 2627584 | tf_op jit(solution)/shard_map/while/body/eval_jaxpr/cond/branch_1_fun/convert_element_type | solution.py:34
  68.2 6.3 %collective-permute-done.1 = f32[512]{0:T(512)S(1)} collective-permute-done((f32[512]{0:T(512)S(1)}, f32[512]{0:T(512)S(1)}, u32[]{:S(2)}, u32[]{:S(2)}) %collective-permute-start.1) | collective-permute-done | bytes 2080 | tf_op jit(solution)/shard_map/while/body/eval_jaxpr/ppermute | solution.py:11
  74.5 0.8 %fusion.19 = bf16[1,512,128]{2,1,0:T(8,128)(2,1)} fusion(f32[512,128]{1,0:T(8,128)S(1)} %get-tuple-element.297, f32[512,128]{1,0:T(8,128)S(1)} %get-tuple-element.299, f32[512]{0:T(512)S(1)} %negate_exponential_fusion.1), kind=kLoop, calls=%fused_computation.41 | loop fusion | flops 196608 | bytes 657408 | tf_op jit(solution)/shard_map/stack | solution.py:70
  (54 shorter events, 4.1 us)
Async XLA Ops:
  7.8 1.5 %copy-start.1 = (bf16[512,128]{1,0:T(8,128)(2,1)S(1)}, bf16[512,128]{1,0:T(8,128)(2,1)}, u32[]{:S(2)}) copy-start(bf16[512,128]{1,0:T(8,128)(2,1)} %get-tuple-element.274) | copy-start | bytes 393220 | tf_op jit(solution)/shard_map/cond
  27.4 0.9 %copy-start = (bf16[1,512,128]{2,1,0:T(8,128)(2,1)S(1)}, bf16[1,512,128]{2,1,0:T(8,128)(2,1)}, u32[]{:S(2)}) copy-start(bf16[1,512,128]{2,1,0:T(8,128)(2,1)} %param.12) | copy-start | bytes 393220
  27.4 1.0 %copy-start.2 = (bf16[1,512,128]{2,1,0:T(8,128)(2,1)S(1)}, bf16[1,512,128]{2,1,0:T(8,128)(2,1)}, u32[]{:S(2)}) copy-start(bf16[1,512,128]{2,1,0:T(8,128)(2,1)} %param.11) | copy-start | bytes 393220
  37.2 6.8 %collective-permute-start = (f32[512,128]{1,0:T(8,128)S(1)}, f32[512,128]{1,0:T(8,128)S(1)}, u32[]{:S(2)}, u32[]{:S(2)}) collective-permute-start(f32[512,128]{1,0:T(8,128)S(1)} %multiply_add_fusion.2), channel_id=1, source_target_pairs={{4,0},{8,4},{12,8},{0,12},{5,1},{9,5},{13,9},{1,13},{6,2},{10,6},{... | collective-permute-start | bytes 786440 | tf_op jit(solution)/shard_map/while/body/eval_jaxpr/ppermute | solution.py:11
  37.3 6.7 %collective-permute-start.1 = (f32[512]{0:T(512)S(1)}, f32[512]{0:T(512)S(1)}, u32[]{:S(2)}, u32[]{:S(2)}) collective-permute-start(f32[512]{0:T(512)S(1)} %get-tuple-element.392), channel_id=1, source_target_pairs={{4,0},{8,4},{12,8},{0,12},{5,1},{9,5},{13,9},{1,13},{6,2},{10,6},{... | collective-permute-start | bytes 6152 | tf_op jit(solution)/shard_map/while/body/eval_jaxpr/ppermute | solution.py:11
  52.8 6.5 %collective-permute-start = (f32[512,128]{1,0:T(8,128)S(1)}, f32[512,128]{1,0:T(8,128)S(1)}, u32[]{:S(2)}, u32[]{:S(2)}) collective-permute-start(f32[512,128]{1,0:T(8,128)S(1)} %multiply_add_fusion.2), channel_id=1, source_target_pairs={{4,0},{8,4},{12,8},{0,12},{5,1},{9,5},{13,9},{1,13},{6,2},{10,6},{... | collective-permute-start | bytes 786440 | tf_op jit(solution)/shard_map/while/body/eval_jaxpr/ppermute | solution.py:11
  52.9 6.4 %collective-permute-start.1 = (f32[512]{0:T(512)S(1)}, f32[512]{0:T(512)S(1)}, u32[]{:S(2)}, u32[]{:S(2)}) collective-permute-start(f32[512]{0:T(512)S(1)} %get-tuple-element.392), channel_id=1, source_target_pairs={{4,0},{8,4},{12,8},{0,12},{5,1},{9,5},{13,9},{1,13},{6,2},{10,6},{... | collective-permute-start | bytes 6152 | tf_op jit(solution)/shard_map/while/body/eval_jaxpr/ppermute | solution.py:11
  68.1 6.5 %collective-permute-start = (f32[512,128]{1,0:T(8,128)S(1)}, f32[512,128]{1,0:T(8,128)S(1)}, u32[]{:S(2)}, u32[]{:S(2)}) collective-permute-start(f32[512,128]{1,0:T(8,128)S(1)} %multiply_add_fusion.2), channel_id=1, source_target_pairs={{4,0},{8,4},{12,8},{0,12},{5,1},{9,5},{13,9},{1,13},{6,2},{10,6},{... | collective-permute-start | bytes 786440 | tf_op jit(solution)/shard_map/while/body/eval_jaxpr/ppermute | solution.py:11
  68.2 6.4 %collective-permute-start.1 = (f32[512]{0:T(512)S(1)}, f32[512]{0:T(512)S(1)}, u32[]{:S(2)}, u32[]{:S(2)}) collective-permute-start(f32[512]{0:T(512)S(1)} %get-tuple-element.392), channel_id=1, source_target_pairs={{4,0},{8,4},{12,8},{0,12},{5,1},{9,5},{13,9},{1,13},{6,2},{10,6},{... | collective-permute-start | bytes 6152 | tf_op jit(solution)/shard_map/while/body/eval_jaxpr/ppermute | solution.py:11
where the time goes:
time: 75.5 us; the launch traced here: 75.3 us
  other arithmetic  26.9 us (36%)
  blocking collectives  17.8 us (24%)
  waiting for transfers between devices  17.1 us (23%)
  matrix products  8.32 us (11%)
  starting transfers between devices  2.47 us (3%)
  local copies, waits for them, and re-layouts  2.38 us (3%)
    another operation x8, other arithmetic  19.3 us
    all_gather x1, blocking collectives, one_head(): lax.all_gather(q_own, 'ctx', axis=0, tiled=True).reshape(count, rows, width)  17.8 us
    ppermute x6, waiting for transfers between devices, shifted(): return lax.ppermute(block, axis, route)  17.1 us
    dot_general x4, matrix products, compute(): lax.dot_general(qrows, kblock, (((1,), (1,)), ((), ())), preferred_elemen...  6.95 us
    convert_element_type x4, other arithmetic, compute(): jnp.where(live, jnp.exp(jax.nn.log_sigmoid(score) - later), 0.0)  5.99 us
    ppermute x6, starting transfers between devices, shifted(): return lax.ppermute(block, axis, route)  2.47 us
  transfers between devices with their start and end apart: 6, of which 3 were waited for; matrix products, arithmetic and copies ran while one was open for 0% of the time, Pallas kernels for 0%

commit v1 on v0

--- a/solution.py
+++ b/solution.py
@@ -3,6 +3,24 @@
 import jax.numpy as jnp
 from jax import lax
 from jax.sharding import PartitionSpec as P
+
+
+def collect(value, axis, dim):
+    ways, here, lap = (lax.axis_size(axis), lax.axis_index(axis), value.shape[dim])
+    dims = [n * ways if d == dim else n for d, n in enumerate(value.shape)]
+    full = lax.dynamic_update_slice_in_dim(
+        jnp.zeros(dims, value.dtype), value, here * lap, axis=dim
+    )
+    going_up = going_down = value
+    for far in range(1, ways // 2 + 1):
+        going_up = lax.ppermute(going_up, axis, [(d, (d + 1) % ways) for d in range(ways)])
+        full = lax.dynamic_update_slice_in_dim(full, going_up, (here - far) % ways * lap, axis=dim)
+        if 2 * far < ways:
+            going_down = lax.ppermute(going_down, axis, [(d, (d - 1) % ways) for d in range(ways)])
+            full = lax.dynamic_update_slice_in_dim(
+                full, going_down, (here + far) % ways * lap, axis=dim
+            )
+    return full
 
 
 def shifted(block, axis, distance):
@@ -47,7 +65,7 @@
     count = lax.axis_size("ctx")
     place = lax.axis_index("ctx")
     own_start = place * rows
-    gathered = lax.all_gather(q_own, "ctx", axis=0, tiled=True).reshape(count, rows, width)
+    gathered = collect(q_own, "ctx", 0).reshape(count, rows, width)
 
     def advance(step, message):
         summed, spent_sum = message

time: 75.5 us -> 69.9 us (0.926)
  blocking collectives: 17.8 us -> 0 us
  waiting for transfers between devices: 17.1 us -> 25 us
  starting transfers between devices: 2.47 us -> 6.27 us
  local copies, waits for them, and re-layouts: 2.38 us -> 3.68 us
  matrix products: 8.32 us -> 7.35 us
    all_gather x1 -> x0, blocking collectives: 17.8 us -> none  [one_head(): lax.all_gather(q_own, 'ctx', axis=0, tiled=True).reshape(count, rows, width)]
    ppermute x0 -> x3, waiting for transfers between devices: none -> 6.4 us  [the longest x2 6.4 us: collect(): lax.ppermute(going_up, axis, [(d, (d + 1) % ways) for d in range(ways)])]
    ppermute x0 -> x3, starting transfers between devices: none -> 5.32 us  [the longest x2 3.29 us: collect(): lax.ppermute(going_up, axis, [(d, (d + 1) % ways) for d in range(ways)])]
    ppermute x6, starting transfers between devices: 2.47 us -> 0.95 us  [shifted(): return lax.ppermute(block, axis, route)]
    ppermute x6, waiting for transfers between devices: 17.1 us -> 18.6 us  [shifted(): return lax.ppermute(block, axis, route)]
    unnamed x4 -> x10, local copies, waits for them, and re-layouts: 0.94 us -> 2.1 us
    dot_general x4, matrix products: 6.95 us -> 5.99 us  [compute(): lax.dot_general(qrows, kblock, (((1,), (1,)), ((), ())), preferred_elemen...]
  transfers between devices with their start and end apart: 6 -> 9, of which waited for: 3 -> 4; matrix products, arithmetic and copies ran while one was open for 0% -> 13% of each run, Pallas kernels for 0% -> 0%
where the time goes in v1:
time: 69.9 us; the launch traced here: 69.8 us
  other arithmetic  26.9 us (38%)
  waiting for transfers between devices  25 us (36%)
  matrix products  7.35 us (11%)
  starting transfers between devices  6.27 us (9%)
  local copies, waits for them, and re-layouts  3.68 us (5%)
    another operation x8, other arithmetic  19.3 us
    ppermute x6, waiting for transfers between devices, shifted(): return lax.ppermute(block, axis, route)  18.6 us
    ppermute x2, waiting for transfers between devices, collect(): lax.ppermute(going_up, axis, [(d, (d + 1) % ways) for d in range(ways)])  6.4 us
    convert_element_type x4, other arithmetic, compute(): jnp.where(live, jnp.exp(jax.nn.log_sigmoid(score) - later), 0.0)  5.99 us
    dot_general x4, matrix products, compute(): lax.dot_general(qrows, kblock, (((1,), (1,)), ((), ())), preferred_elemen...  5.99 us
    ppermute x2, starting transfers between devices, collect(): lax.ppermute(going_up, axis, [(d, (d + 1) % ways) for d in range(ways)])  3.29 us
    unnamed x10, local copies, waits for them, and re-layouts  2.1 us
    ppermute x1, starting transfers between devices, collect(): lax.ppermute(going_down, axis, [(d, (d - 1) % ways) for d in range(ways)])  2.03 us
  transfers between devices with their start and end apart: 9, of which 4 were waited for; matrix products, arithmetic and copies ran while one was open for 13% of the time, Pallas kernels for 0%

profile of v1, /device:TPU:0, one launch (start us, length us, event | category | flops | bytes accessed | tf_op | source)
XLA Modules:
  0.0 69.8 jit_solution(4348678397589914659)
XLA Ops:
  0.0 3.1 %collective-permute-start.2 = (bf16[512,128]{1,0:T(8,128)(2,1)}, bf16[512,128]{1,0:T(8,128)(2,1)S(1)}, u32[]{:S(2)}, u32[]{:S(2)}) collective-permute-start(bf16[512,128]{1,0:T(8,128)(2,1)} %bitcast.50), channel_id=1, source_target_pairs={{0,4},{4,8},{8,12},{12,0},{1,5},{5,9},{9,13},{13,1},{2,6},{6,10},{... | collective-permute-start | bytes 393224 | tf_op jit(solution)/shard_map/ppermute | solution.py:16
  3.1 2.0 %collective-permute-start.3 = (bf16[512,128]{1,0:T(8,128)(2,1)}, bf16[512,128]{1,0:T(8,128)(2,1)S(1)}, u32[]{:S(2)}, u32[]{:S(2)}) collective-permute-start(bf16[512,128]{1,0:T(8,128)(2,1)} %bitcast.51), channel_id=1, source_target_pairs={{0,12},{4,0},{8,4},{12,8},{1,13},{5,1},{9,5},{13,9},{2,14},{6,2},{... | collective-permute-start | bytes 393224 | tf_op jit(solution)/shard_map/ppermute | solution.py:19
  6.0 0.9 %copy-done = bf16[1,512,128]{2,1,0:T(8,128)(2,1)S(1)} copy-done((bf16[1,512,128]{2,1,0:T(8,128)(2,1)S(1)}, bf16[1,512,128]{2,1,0:T(8,128)(2,1)}, u32[]{:S(2)}) %copy-start) | copy-done | bytes 131096
  7.0 8.7 %conditional.2 = (f32[512]{0:T(512)S(1)}, f32[512,128]{1,0:T(8,128)S(1)}) conditional(s32[]{:T(128)} %convert_element_type.23, () %tuple.48, (s32[]{:T(128)}, bf16[512,128]{1,0:T(8,128)(2,1)S(1)}, bf16[512,128]{1,0:T(8,128)(2,1)S(1)}, f32[]{:T(128)}, bf16[512,128]{1,0:T(8,128)(2,1)S(1)}) %tuple.82), branch_computations={%region_0.1_spmd, %region_1.5_spmd} | conditional | flops 175906304 | bytes 12290076 | solution.py:60
  7.0 1.5 %compare_select_fusion.3 = (f32[512,512]{0,1:T(8,128)S(1)}, f32[512,512]{0,1:T(8,128)S(1)}) fusion(s32[512]{0:T(512)S(1)} %iota_add_fusion, f32[]{:T(128)} %get-tuple-element.273, bf16[512,128]{1,0:T(8,128)(2,1)S(1)} %get-tuple-element.271, bf16[512,128]{1,0:T(8,128)(2,1)S(1)} %get-tuple-element.272), kind=kOutput, calls=%fused_computation.5 | convolution fusion | flops 69730304 | bytes 2361348 | tf_op jit(solution)/shard_map/cond/branch_1_fun/dot_general | solution.py:40
  8.5 4.8 %fusion.5 = f32[512,4,128]{0,1,2:T(4,128)S(1)} fusion(f32[512,4,128]{0,2,1:T(8,128)S(1)} %bitcast.48), kind=kOutput, calls=%fused_computation.11 | output fusion | flops 33292288 | bytes 2097152 | tf_op jit(solution)/shard_map/reduce-window.2
  13.8 1.5 %fusion.1 = (bf16[512,512]{0,1:T(8,128)(2,1)S(1)}, f32[512]{0:T(512)S(1)}) fusion(f32[512,4,128]{0,2,1:T(8,128)S(1)} %copy.6, f32[512,512]{0,1:T(8,128)S(1)} %get-tuple-element.321, s32[512]{0:T(512)S(1)} %iota_add_fusion), kind=kLoop, calls=%fused_computation.6 | loop fusion | flops 5504512 | bytes 2625536 | tf_op jit(solution)/shard_map/cond/branch_1_fun/convert_element_type | solution.py:52
  16.3 6.4 %collective-permute-done.4 = bf16[512,128]{1,0:T(8,128)(2,1)S(1)} collective-permute-done((bf16[512,128]{1,0:T(8,128)(2,1)S(1)}, bf16[512,128]{1,0:T(8,128)(2,1)S(1)}, u32[]{:S(2)}, u32[]{:S(2)}) %collective-permute-start.4) | collective-permute-done | bytes 131104 | tf_op jit(solution)/shard_map/ppermute | solution.py:16
  22.8 46.2 %while.17 = (s32[]{:T(128)}, f32[512,128]{1,0:T(8,128)S(1)}, f32[512]{0:T(512)S(1)}, s32[]{:T(128)}, s32[]{:T(128)}, /*index=5*/bf16[4,512,128]{2,1,0:T(8,128)(2...) while((s32[]{:T(128)}, f32[512,128]{1,0:T(8,128)S(1)}, ...), condition=%wide.region_11.12_spmd, body=%wide.region_5.11_spmd.sunk | while | flops 176038928 | bytes 14150142 | solution.py:80
  22.8 8.7 %conditional.4 = (f32[512]{0:T(512)S(1)}, f32[512,128]{1,0:T(8,128)S(1)}) conditional(s32[]{:T(128)} %convert_element_type.31, () %tuple.69, (s32[]{:T(128)}, s32[]{:T(128)}, s32[]{:T(128)}, bf16[4,512,128]{2,1,0:T(8,128)(2,1)S(1)}, bf16[512,128]{1,0:T(8,128)(2,1)S(1)}, /*index=5*/f32[]{:T(128)}, bf16[512,128]{1,0:T(8,128)(2,1)S(1)}) %tuple.70), branch_computations={%region_6.6_spmd, %region_7.10_spmd} | conditional | flops 175906816 | bytes 12296262 | solution.py:60
  22.9 1.5 %compare_select_fusion.7 = (f32[512,512]{0,1:T(8,128)S(1)}, f32[512,512]{0,1:T(8,128)S(1)}) fusion(s32[512]{0:T(512)S(1)} %get-tuple-element.326, s32[512]{0:T(512)S(1)} %get-tuple-element.327, f32[]{:T(128)} %get-tuple-element.280, bf16[512,128]{1,0:T(8,128)(2,1)S(1)} %get-tuple-element.279, bf16[4,512,128]{2,1,0:T(8,128)(2,1)S(1)} %get-tuple-element.277, ...), kind=kOutput, calls=%fused_computation.22 | convolution fusion | flops 69730304 | bytes 2363400 | tf_op jit(solution)/shard_map/while/body/eval_jaxpr/cond/branch_1_fun/dot_general | solution.py:40
  24.4 4.8 %fusion.13 = f32[512,4,128]{0,1,2:T(4,128)S(1)} fusion(f32[512,4,128]{0,2,1:T(8,128)S(1)} %bitcast.42), kind=kOutput, calls=%fused_computation.28 | output fusion | flops 33292288 | bytes 2097152 | tf_op jit(solution)/shard_map/reduce-window.4
  29.7 1.5 %fusion.9 = (bf16[512,512]{0,1:T(8,128)(2,1)S(1)}, f32[512]{0:T(512)S(1)}) fusion(f32[512,4,128]{0,2,1:T(8,128)S(1)} %copy.8, f32[512,512]{0,1:T(8,128)S(1)} %get-tuple-element.325, s32[512]{0:T(512)S(1)} %get-tuple-element.326, s32[512]{0:T(512)S(1)} %get-tuple-element.327), kind=kLoop, calls=%fused_computation.23 | loop fusion | flops 5504512 | bytes 2627584 | tf_op jit(solution)/shard_map/while/body/eval_jaxpr/cond/branch_1_fun/convert_element_type | solution.py:52
  32.4 6.0 %collective-permute-done.1 = f32[512]{0:T(512)S(1)} collective-permute-done((f32[512]{0:T(512)S(1)}, f32[512]{0:T(512)S(1)}, u32[]{:S(2)}, u32[]{:S(2)}) %collective-permute-start.1) | collective-permute-done | bytes 2080 | tf_op jit(solution)/shard_map/while/body/eval_jaxpr/ppermute | solution.py:29
  38.4 8.7 %conditional.4 = (f32[512]{0:T(512)S(1)}, f32[512,128]{1,0:T(8,128)S(1)}) conditional(s32[]{:T(128)} %convert_element_type.31, () %tuple.69, (s32[]{:T(128)}, s32[]{:T(128)}, s32[]{:T(128)}, bf16[4,512,128]{2,1,0:T(8,128)(2,1)S(1)}, bf16[512,128]{1,0:T(8,128)(2,1)S(1)}, /*index=5*/f32[]{:T(128)}, bf16[512,128]{1,0:T(8,128)(2,1)S(1)}) %tuple.70), branch_computations={%region_6.6_spmd, %region_7.10_spmd} | conditional | flops 175906816 | bytes 12296262 | solution.py:60
  38.4 1.5 %compare_select_fusion.7 = (f32[512,512]{0,1:T(8,128)S(1)}, f32[512,512]{0,1:T(8,128)S(1)}) fusion(s32[512]{0:T(512)S(1)} %get-tuple-element.326, s32[512]{0:T(512)S(1)} %get-tuple-element.327, f32[]{:T(128)} %get-tuple-element.280, bf16[512,128]{1,0:T(8,128)(2,1)S(1)} %get-tuple-element.279, bf16[4,512,128]{2,1,0:T(8,128)(2,1)S(1)} %get-tuple-element.277, ...), kind=kOutput, calls=%fused_computation.22 | convolution fusion | flops 69730304 | bytes 2363400 | tf_op jit(solution)/shard_map/while/body/eval_jaxpr/cond/branch_1_fun/dot_general | solution.py:40
  39.9 4.8 %fusion.13 = f32[512,4,128]{0,1,2:T(4,128)S(1)} fusion(f32[512,4,128]{0,2,1:T(8,128)S(1)} %bitcast.42), kind=kOutput, calls=%fused_computation.28 | output fusion | flops 33292288 | bytes 2097152 | tf_op jit(solution)/shard_map/reduce-window.4
  45.2 1.5 %fusion.9 = (bf16[512,512]{0,1:T(8,128)(2,1)S(1)}, f32[512]{0:T(512)S(1)}) fusion(f32[512,4,128]{0,2,1:T(8,128)S(1)} %copy.8, f32[512,512]{0,1:T(8,128)S(1)} %get-tuple-element.325, s32[512]{0:T(512)S(1)} %get-tuple-element.326, s32[512]{0:T(512)S(1)} %get-tuple-element.327), kind=kLoop, calls=%fused_computation.23 | loop fusion | flops 5504512 | bytes 2627584 | tf_op jit(solution)/shard_map/while/body/eval_jaxpr/cond/branch_1_fun/convert_element_type | solution.py:52
  47.4 6.3 %collective-permute-done.1 = f32[512]{0:T(512)S(1)} collective-permute-done((f32[512]{0:T(512)S(1)}, f32[512]{0:T(512)S(1)}, u32[]{:S(2)}, u32[]{:S(2)}) %collective-permute-start.1) | collective-permute-done | bytes 2080 | tf_op jit(solution)/shard_map/while/body/eval_jaxpr/ppermute | solution.py:29
  53.7 8.7 %conditional.4 = (f32[512]{0:T(512)S(1)}, f32[512,128]{1,0:T(8,128)S(1)}) conditional(s32[]{:T(128)} %convert_element_type.31, () %tuple.69, (s32[]{:T(128)}, s32[]{:T(128)}, s32[]{:T(128)}, bf16[4,512,128]{2,1,0:T(8,128)(2,1)S(1)}, bf16[512,128]{1,0:T(8,128)(2,1)S(1)}, /*index=5*/f32[]{:T(128)}, bf16[512,128]{1,0:T(8,128)(2,1)S(1)}) %tuple.70), branch_computations={%region_6.6_spmd, %region_7.10_spmd} | conditional | flops 175906816 | bytes 12296262 | solution.py:60
  53.7 1.5 %compare_select_fusion.7 = (f32[512,512]{0,1:T(8,128)S(1)}, f32[512,512]{0,1:T(8,128)S(1)}) fusion(s32[512]{0:T(512)S(1)} %get-tuple-element.326, s32[512]{0:T(512)S(1)} %get-tuple-element.327, f32[]{:T(128)} %get-tuple-element.280, bf16[512,128]{1,0:T(8,128)(2,1)S(1)} %get-tuple-element.279, bf16[4,512,128]{2,1,0:T(8,128)(2,1)S(1)} %get-tuple-element.277, ...), kind=kOutput, calls=%fused_computation.22 | convolution fusion | flops 69730304 | bytes 2363400 | tf_op jit(solution)/shard_map/while/body/eval_jaxpr/cond/branch_1_fun/dot_general | solution.py:40
  55.2 4.8 %fusion.13 = f32[512,4,128]{0,1,2:T(4,128)S(1)} fusion(f32[512,4,128]{0,2,1:T(8,128)S(1)} %bitcast.42), kind=kOutput, calls=%fused_computation.28 | output fusion | flops 33292288 | bytes 2097152 | tf_op jit(solution)/shard_map/reduce-window.4
  60.5 1.5 %fusion.9 = (bf16[512,512]{0,1:T(8,128)(2,1)S(1)}, f32[512]{0:T(512)S(1)}) fusion(f32[512,4,128]{0,2,1:T(8,128)S(1)} %copy.8, f32[512,512]{0,1:T(8,128)S(1)} %get-tuple-element.325, s32[512]{0:T(512)S(1)} %get-tuple-element.326, s32[512]{0:T(512)S(1)} %get-tuple-element.327), kind=kLoop, calls=%fused_computation.23 | loop fusion | flops 5504512 | bytes 2627584 | tf_op jit(solution)/shard_map/while/body/eval_jaxpr/cond/branch_1_fun/convert_element_type | solution.py:52
  62.6 6.3 %collective-permute-done.1 = f32[512]{0:T(512)S(1)} collective-permute-done((f32[512]{0:T(512)S(1)}, f32[512]{0:T(512)S(1)}, u32[]{:S(2)}, u32[]{:S(2)}) %collective-permute-start.1) | collective-permute-done | bytes 2080 | tf_op jit(solution)/shard_map/while/body/eval_jaxpr/ppermute | solution.py:29
  (68 shorter events, 7.1 us)
Async XLA Ops:
  0.0 15.7 %collective-permute-start.2 = (bf16[512,128]{1,0:T(8,128)(2,1)}, bf16[512,128]{1,0:T(8,128)(2,1)S(1)}, u32[]{:S(2)}, u32[]{:S(2)}) collective-permute-start(bf16[512,128]{1,0:T(8,128)(2,1)} %bitcast.50), channel_id=1, source_target_pairs={{0,4},{4,8},{8,12},{12,0},{1,5},{5,9},{9,13},{13,1},{2,6},{6,10},{... | collective-permute-start | bytes 393224 | tf_op jit(solution)/shard_map/ppermute | solution.py:16
  3.1 13.0 %collective-permute-start.3 = (bf16[512,128]{1,0:T(8,128)(2,1)}, bf16[512,128]{1,0:T(8,128)(2,1)S(1)}, u32[]{:S(2)}, u32[]{:S(2)}) collective-permute-start(bf16[512,128]{1,0:T(8,128)(2,1)} %bitcast.51), channel_id=1, source_target_pairs={{0,12},{4,0},{8,4},{12,8},{1,13},{5,1},{9,5},{13,9},{2,14},{6,2},{... | collective-permute-start | bytes 393224 | tf_op jit(solution)/shard_map/ppermute | solution.py:19
  5.1 0.9 %copy-start.3 = (bf16[1,512,128]{2,1,0:T(8,128)(2,1)S(1)}, bf16[1,512,128]{2,1,0:T(8,128)(2,1)}, u32[]{:S(2)}) copy-start(bf16[1,512,128]{2,1,0:T(8,128)(2,1)} %param.10) | copy-start | bytes 393220
  6.0 0.9 %copy-start = (bf16[1,512,128]{2,1,0:T(8,128)(2,1)S(1)}, bf16[1,512,128]{2,1,0:T(8,128)(2,1)}, u32[]{:S(2)}) copy-start(bf16[1,512,128]{2,1,0:T(8,128)(2,1)} %param.12) | copy-start | bytes 393220
  6.0 1.0 %copy-start.4 = (bf16[1,512,128]{2,1,0:T(8,128)(2,1)S(1)}, bf16[1,512,128]{2,1,0:T(8,128)(2,1)}, u32[]{:S(2)}) copy-start(bf16[1,512,128]{2,1,0:T(8,128)(2,1)} %param.11) | copy-start | bytes 393220
  15.6 0.7 copy-start.1
  15.7 7.0 %collective-permute-start.4 = (bf16[512,128]{1,0:T(8,128)(2,1)S(1)}, bf16[512,128]{1,0:T(8,128)(2,1)S(1)}, u32[]{:S(2)}, u32[]{:S(2)}) collective-permute-start(bf16[512,128]{1,0:T(8,128)(2,1)S(1)} %collective-permute-done.2), channel_id=1, source_target_pairs={{0,4},{4,8},{8,12},{12,0},{1,5},{5,9},{9,13},{13,1},{2,6},{6,10},{... | collective-permute-start | bytes 393224 | tf_op jit(solution)/shard_map/ppermute | solution.py:16
  22.8 46.2 %copy-start.2 = (f32[512,128]{1,0:T(8,128)S(1)}, f32[512,128]{1,0:T(8,128)}, u32[]{:S(2)}) copy-start(f32[512,128]{1,0:T(8,128)} %copy-done.1) | copy-start | bytes 786436
  31.7 6.7 %collective-permute-start = (f32[512,128]{1,0:T(8,128)S(1)}, f32[512,128]{1,0:T(8,128)S(1)}, u32[]{:S(2)}, u32[]{:S(2)}) collective-permute-start(f32[512,128]{1,0:T(8,128)S(1)} %multiply_add_fusion.2), channel_id=1, source_target_pairs={{4,0},{8,4},{12,8},{0,12},{5,1},{9,5},{13,9},{1,13},{6,2},{10,6},{... | collective-permute-start | bytes 786440 | tf_op jit(solution)/shard_map/while/body/eval_jaxpr/ppermute | solution.py:29
  31.8 6.6 %collective-permute-start.1 = (f32[512]{0:T(512)S(1)}, f32[512]{0:T(512)S(1)}, u32[]{:S(2)}, u32[]{:S(2)}) collective-permute-start(f32[512]{0:T(512)S(1)} %get-tuple-element.392), channel_id=1, source_target_pairs={{4,0},{8,4},{12,8},{0,12},{5,1},{9,5},{13,9},{1,13},{6,2},{10,6},{... | collective-permute-start | bytes 6152 | tf_op jit(solution)/shard_map/while/body/eval_jaxpr/ppermute | solution.py:29
  47.2 6.5 %collective-permute-start = (f32[512,128]{1,0:T(8,128)S(1)}, f32[512,128]{1,0:T(8,128)S(1)}, u32[]{:S(2)}, u32[]{:S(2)}) collective-permute-start(f32[512,128]{1,0:T(8,128)S(1)} %multiply_add_fusion.2), channel_id=1, source_target_pairs={{4,0},{8,4},{12,8},{0,12},{5,1},{9,5},{13,9},{1,13},{6,2},{10,6},{... | collective-permute-start | bytes 786440 | tf_op jit(solution)/shard_map/while/body/eval_jaxpr/ppermute | solution.py:29
  47.3 6.4 %collective-permute-start.1 = (f32[512]{0:T(512)S(1)}, f32[512]{0:T(512)S(1)}, u32[]{:S(2)}, u32[]{:S(2)}) collective-permute-start(f32[512]{0:T(512)S(1)} %get-tuple-element.392), channel_id=1, source_target_pairs={{4,0},{8,4},{12,8},{0,12},{5,1},{9,5},{13,9},{1,13},{6,2},{10,6},{... | collective-permute-start | bytes 6152 | tf_op jit(solution)/shard_map/while/body/eval_jaxpr/ppermute | solution.py:29
  62.5 6.5 %collective-permute-start = (f32[512,128]{1,0:T(8,128)S(1)}, f32[512,128]{1,0:T(8,128)S(1)}, u32[]{:S(2)}, u32[]{:S(2)}) collective-permute-start(f32[512,128]{1,0:T(8,128)S(1)} %multiply_add_fusion.2), channel_id=1, source_target_pairs={{4,0},{8,4},{12,8},{0,12},{5,1},{9,5},{13,9},{1,13},{6,2},{10,6},{... | collective-permute-start | bytes 786440 | tf_op jit(solution)/shard_map/while/body/eval_jaxpr/ppermute | solution.py:29
  62.6 6.4 %collective-permute-start.1 = (f32[512]{0:T(512)S(1)}, f32[512]{0:T(512)S(1)}, u32[]{:S(2)}, u32[]{:S(2)}) collective-permute-start(f32[512]{0:T(512)S(1)} %get-tuple-element.392), channel_id=1, source_target_pairs={{4,0},{8,4},{12,8},{0,12},{5,1},{9,5},{13,9},{1,13},{6,2},{10,6},{... | collective-permute-start | bytes 6152 | tf_op jit(solution)/shard_map/while/body/eval_jaxpr/ppermute | solution.py:29
